TPU v7x, 32 devices: a whole 2x2x4 slice. The times are simulated.
32 devices in a mesh: groups: 2 (over y), feat: 4 (over z), tower: 4 (over x, core).
Axes of the slice: x: 2, y: 2, z: 4, core: 2. Of those that a mesh axis runs over, the one named last changes fastest.
Arguments:
- pooled_first: bfloat16 [4, 16, 3072, 128], P('tower', 'feat', 'groups'), parts along dimension 2, may hold values from -6 to 6
- pooled_second: bfloat16 [4, 16, 3072, 128], P('tower', 'feat', 'groups'), parts along dimension 2, may hold values from -6 to 6
- feature_order: int32 [4, 32], P('tower'), may hold values from 0 to 31, each once within a row
- cross_down: bfloat16 [4, 4096, 256], P('tower', 'feat'), may hold values from -0.09375 to 0.09375
- cross_up: bfloat16 [4, 4096, 256], P('tower', 'feat'), may hold values from -0.375 to 0.375
- cross_bias: float32 [4, 4096], P('tower'), may hold values from -3 to 3
- compress_weight: bfloat16 [4, 4096, 512], P('tower', 'feat'), may hold values from -0.09375 to 0.09375
- compress_bias: float32 [4, 512], P('tower'), may hold values from -3 to 3
- dense_vector: bfloat16 [3072, 128], P(('groups', 'feat', 'tower')), parts along dimension 0, may hold values from -6 to 6
- mlp_weight: bfloat16 [248, 1024], P('tower'), may hold values from -0.375 to 0.375
- mlp_bias: float32 [1024], replicated, may hold values from -3 to 3
Outputs:
- top_hidden: bfloat16 [3072, 1024], P(('groups', 'feat', 'tower')), parts along dimension 0
There are 2 independent parts, one for each index of `groups`. A program takes and returns all parts, laid end to end along the dimension named above; an argument that names none is the same for every part. Nothing has to cross between parts.
Inputs may be any that keep to these rules, and one draw needn't show every extreme that they name: Each row of feature_order names every number from 0 to 31 once.
All inputs are finite; a program needn't handle non-finite values.
Results may differ from a plain program's by a relative error of at most 0.0072.
Values may be sent and summed in bfloat16 or wider, within the bound.
No kernel may reach another device: no remote copies, remote signals or barrier semaphores. Data moves between devices by JAX's collectives and lax.ppermute only.
A program may use at most 64 MiB of HBM per device.

v0:
```python
import math
import jax
import jax.numpy as jnp
import numpy as np
from jax import lax
from jax.sharding import PartitionSpec as P


def pair_positions(vector_count):
    upper_rows, upper_cols = np.triu_indices(vector_count, 1)
    return upper_rows * vector_count + upper_cols


def on_device(
    pooled_first,
    pooled_second,
    feature_order,
    cross_down,
    cross_up,
    cross_bias,
    compress_weight,
    compress_bias,
    dense_vector,
    mlp_weight,
    mlp_bias,
):
    group_one, group_two = (
        lax.all_to_all(pooled_first, "feat", split_axis=2, concat_axis=1, tiled=True),
        lax.all_to_all(pooled_second, "feat", split_axis=2, concat_axis=1, tiled=True),
    )
    slot_data = jnp.concatenate([group_one[0], group_two[0]], 0)
    slot_count = slot_data.shape[0]
    row_count = slot_data.shape[1]
    entry_count = slot_data.shape[2]
    orders = feature_order[0]
    one_hot = (orders[None, :] == jnp.arange(slot_count, dtype=jnp.int32)[:, None]).astype(
        jnp.bfloat16
    )
    base_rows = jnp.einsum("fs,sre->rfe", one_hot, slot_data, preferred_element_type=jnp.float32)
    base_rows = base_rows.astype(jnp.bfloat16).reshape(row_count, slot_count * entry_count)
    weight_piece = lax.all_gather(cross_down[0], "feat", axis=0, tiled=True)
    columns = base_rows
    low_sum = jnp.dot(columns, weight_piece, preferred_element_type=jnp.float32)
    low_rank = low_sum.astype(jnp.bfloat16)
    shift_row = cross_bias[0]
    up_piece = lax.all_gather(cross_up[0], "feat", axis=0, tiled=True)
    squeeze_piece = lax.all_gather(compress_weight[0], "feat", axis=0, tiled=True)
    lifted = lax.dot_general(
        low_rank, up_piece, (((1,), (1,)), ((), ())), preferred_element_type=jnp.float32
    )
    columns = base_rows.astype(jnp.float32)
    crossed = (columns * (lifted + shift_row[None, :]) + columns).astype(jnp.bfloat16)
    squeezed = jnp.dot(crossed, squeeze_piece, preferred_element_type=jnp.float32)
    compressed = (squeezed + compress_bias[0][None, :]).astype(jnp.bfloat16)
    gathered = lax.all_to_all(compressed, "tower", split_axis=0, concat_axis=1, tiled=True)
    local_rows = gathered.shape[0]
    vector_count = gathered.shape[1] // entry_count
    vectors = gathered.reshape(local_rows, vector_count, entry_count)
    gram_matrix = jnp.einsum(
        "bie,bje->bij", vectors, vectors, preferred_element_type=jnp.float32
    ) * (1.0 / math.sqrt(entry_count))
    pair_terms = gram_matrix.reshape(local_rows, vector_count * vector_count)[
        :, pair_positions(vector_count)
    ]
    joined = jnp.concatenate([dense_vector.astype(jnp.float32), pair_terms], 1).astype(jnp.bfloat16)
    hidden_units = mlp_weight.shape[1]
    weight_piece = lax.all_gather(mlp_weight, "tower", axis=0, tiled=True)
    width_here = weight_piece.shape[0]
    columns = lax.slice_in_dim(joined, 0, width_here, axis=1)
    hidden_sum = jnp.zeros((local_rows, hidden_units), jnp.float32) + jnp.dot(
        columns, weight_piece, preferred_element_type=jnp.float32
    )
    return jax.nn.relu(hidden_sum + mlp_bias[None, :]).astype(jnp.bfloat16)


def solution(mesh):
    in_specs = (
        P("tower", "feat", "groups", None),
        P("tower", "feat", "groups", None),
        P("tower", None),
        P("tower", "feat", None),
        P("tower", "feat", None),
        P("tower", None),
        P("tower", "feat", None),
        P("tower", None),
        P(("groups", "feat", "tower"), None),
        P("tower", None),
        P(),
    )
    out_specs = P(("groups", "feat", "tower"), None)
    return jax.shard_map(
        on_device, mesh=mesh, in_specs=in_specs, out_specs=out_specs, check_vma=False
    )
```

profile of v0, /device:TPU:0, one launch (start us, length us, event | category | flops | bytes accessed | tf_op | source)
XLA Modules:
  0.0 278.5 jit_solution(6813317362227992565)
XLA Ops:
  6.5 0.7 all-gather.8.cloned.1.call-update
  7.3 0.7 all-gather.10.cloned.1.call-update
  8.1 0.7 all-gather.12.cloned.1.call-update
  8.8 8.2 %copy.24 = bf16[1,4,1536,128]{3,1,0,2:T(4,128)(2,1)} copy(bf16[1,4,1536,128]{3,2,1,0:T(8,128)(2,1)S(1)} %copy-done.2) | data formatting | bytes 3145728 | tf_op args[0]
  17.0 6.3 %all-to-all-start = ((bf16[1,4,1536,128]{3,1,0,2:T(4,128)(2,1)}), bf16[1,4,1536,128]{3,1,0,2:T(4,128)(2,1)S(1)}, u32[]{:S(2)}, u32[]{:S(2)}) async-start(bf16[1,4,1536,128]{3,1,0,2:T(4,128)(2,1)} %copy.24), calls=%async_computation | async-start | bytes 3145728 | tf_op jit(solution)/shard_map/all_to_all | solution.py:28
  23.3 8.2 %copy.26 = bf16[1,4,1536,128]{3,1,0,2:T(4,128)(2,1)} copy(bf16[1,4,1536,128]{3,2,1,0:T(8,128)(2,1)S(1)} %copy-done.3) | data formatting | bytes 3145728 | tf_op args[1]
  31.5 59.2 %all-to-all-done = bf16[1,4,1536,128]{3,1,0,2:T(4,128)(2,1)S(1)} async-done(((bf16[1,4,1536,128]{3,1,0,2:T(4,128)(2,1)}), bf16[1,4,1536,128]{3,1,0,2:T(4,128)(2,1)S(1)}, u32[]{:S(2)}, u32[]{:S(2)}) %all-to-all-start) | async-done | bytes 1572896 | tf_op jit(solution)/shard_map/all_to_all | solution.py:28
  90.7 3.7 %all-to-all-start.1 = ((bf16[1,4,1536,128]{3,1,0,2:T(4,128)(2,1)}), bf16[1,4,1536,128]{3,1,0,2:T(4,128)(2,1)S(1)}, u32[]{:S(2)}, u32[]{:S(2)}) async-start(bf16[1,4,1536,128]{3,1,0,2:T(4,128)(2,1)} %copy.26), calls=%async_computation.1 | async-start | bytes 3145728 | tf_op jit(solution)/shard_map/all_to_all | solution.py:29
  94.5 1.7 copy.25
  96.2 69.1 %all-to-all-done.1 = bf16[1,4,1536,128]{3,1,0,2:T(4,128)(2,1)S(1)} async-done(((bf16[1,4,1536,128]{3,1,0,2:T(4,128)(2,1)}), bf16[1,4,1536,128]{3,1,0,2:T(4,128)(2,1)S(1)}, u32[]{:S(2)}, u32[]{:S(2)}) %all-to-all-start.1) | async-done | bytes 1572896 | tf_op jit(solution)/shard_map/all_to_all | solution.py:29
  165.3 0.5 copy.27
  165.9 2.6 fusion.10
  168.5 3.8 %fusion.23 = bf16[384,256]{1,0:T(8,128)(2,1)S(1)} fusion(bf16[1,4096,256]{2,1,0:T(8,128)(2,1)} %all-gather.8.cloned.1.call-done, bf16[48,8,32,128]{3,2,1,0:T(8,128)(2,1)} %bitcast.56), kind=kOutput, calls=%fused_computation.21 | convolution fusion | flops 805404672 | bytes 5439488 | tf_op jit(solution)/shard_map/dot_general | solution.py:43
  172.3 74.9 %all-gather.12.cloned.1.call-done = bf16[1,4096,512]{2,1,0:T(8,128)(2,1)} async-done(((bf16[1,1024,512]{2,1,0:T(8,128)(2,1)}), bf16[1,4096,512]{2,1,0:T(8,128)(2,1)}) %all-gather.12.cloned.1.call-update) | async-done | bytes 4194320 | tf_op jit(solution)/shard_map/all_gather | solution.py:47
  247.2 7.0 %fusion.18 = bf16[384,512]{1,0:T(8,128)(2,1)} fusion(bf16[1,4096,512]{2,1,0:T(8,128)(2,1)} %all-gather.12.cloned.1.call-done, bf16[384,256]{1,0:T(8,128)(2,1)S(1)} %fusion.23, f32[4096]{0:T(1024)S(1)} %bitcast.63, bf16[48,8,32,128]{3,2,1,0:T(8,128)(2,1)S(1)} %bitcast.57, bf16[1,4096,256]{2,1,0:T(8,128)(2,1)} %all-gather.10.cloned.1.call-done, ...), kind=kOutput, calls=%fused_computation.17 | convolution fusion | flops 2424176640 | bytes 10045440 | tf_op jit(solution)/shard_map/dot_general | solution.py:53
  254.2 3.6 %all-to-all-start.2 = ((bf16[4,96,512]{2,1,0:T(8,128)(2,1)}), bf16[4,96,512]{2,1,0:T(8,128)(2,1)S(1)}, u32[]{:S(2)}, u32[]{:S(2)}) async-start(bf16[4,96,512]{2,1,0:T(8,128)(2,1)} %bitcast.14), calls=%async_computation.2 | async-start | bytes 786432 | tf_op jit(solution)/shard_map/all_to_all | solution.py:55
  257.8 11.1 %all-gather.3 = bf16[4,62,1024]{2,1,0:T(8,128)(2,1)S(1)} all-gather(bf16[1,62,1024]{2,1,0:T(8,128)(2,1)S(1)} %bitcast.60), channel_id=1, replica_groups=mesh['groups'=2,'feat'=4,'tower'=4] {'tower'}, dimensions={0}, use_global_device_ids=true | all-gather | bytes 634880 | tf_op jit(solution)/shard_map/all_gather | solution.py:67
  268.9 0.1 reshape.31
  269.1 0.3 copy.28
  269.4 0.2 reshape.17
  269.5 0.3 convolution_multiply_fusion
  269.9 0.3 copy.29
  270.2 0.7 gather_fusion
  271.1 0.9 fusion.22
  (30 shorter events, 0.3 us)
Async XLA Ops:
  6.5 2.2 copy-start.2
  6.5 162.0 %all-gather.8.cloned.1.call-start = ((), (), s32[]{:S(2)}) async-start(), calls=%async_computation.3 | async-start | bytes 2621440 | tf_op jit(solution)/shard_map/all_gather | solution.py:41
  7.3 165.0 %all-gather.10.cloned.1.call-start = ((), (), s32[]{:S(2)}) async-start(), calls=%async_computation.4 | async-start | bytes 2621440 | tf_op jit(solution)/shard_map/all_gather | solution.py:46
  8.0 239.2 %all-gather.12.cloned.1.call-start = ((), (), s32[]{:S(2)}) async-start(), calls=%async_computation.5 | async-start | bytes 5242880 | tf_op jit(solution)/shard_map/all_gather | solution.py:47
  8.8 14.5 %copy-start.3 = (bf16[1,4,1536,128]{3,2,1,0:T(8,128)(2,1)S(1)}, bf16[1,4,1536,128]{3,2,1,0:T(8,128)(2,1)}, u32[]{:S(2)}) copy-start(bf16[1,4,1536,128]{3,2,1,0:T(8,128)(2,1)} %param.14) | copy-start | bytes 4718596
  17.0 73.7 %all-to-all-start = ((bf16[1,4,1536,128]{3,1,0,2:T(4,128)(2,1)}), bf16[1,4,1536,128]{3,1,0,2:T(4,128)(2,1)S(1)}, u32[]{:S(2)}, u32[]{:S(2)}) async-start(bf16[1,4,1536,128]{3,1,0,2:T(4,128)(2,1)} %copy.24), calls=%async_computation | async-start | bytes 3145728 | tf_op jit(solution)/shard_map/all_to_all | solution.py:28
  90.7 74.6 %all-to-all-start.1 = ((bf16[1,4,1536,128]{3,1,0,2:T(4,128)(2,1)}), bf16[1,4,1536,128]{3,1,0,2:T(4,128)(2,1)S(1)}, u32[]{:S(2)}, u32[]{:S(2)}) async-start(bf16[1,4,1536,128]{3,1,0,2:T(4,128)(2,1)} %copy.26), calls=%async_computation.1 | async-start | bytes 3145728 | tf_op jit(solution)/shard_map/all_to_all | solution.py:29
  94.5 71.4 %copy-start.7 = (s32[1,32]{1,0:T(1,128)S(1)}, s32[1,32]{1,0:T(1,128)}, u32[]{:S(2)}) copy-start(s32[1,32]{1,0:T(1,128)} %param.15) | copy-start | bytes 388
  96.2 69.7 %copy-start = (bf16[1,4,4,384,128]{4,1,2,3,0:T(4,128)(2,1)S(1)}, bf16[1,4,4,384,128]{4,1,2,3,0:T(4,128)(2,1)}, u32[]{:S(2)}) copy-start(bf16[1,4,4,384,128]{4,1,2,3,0:T(4,128)(2,1)} %copy.25) | copy-start | bytes 4718596
  168.5 78.7 %copy-start.1 = (bf16[384,128,32]{1,2,0:T(8,128)(2,1)S(1)}, bf16[384,128,32]{1,2,0:T(8,128)(2,1)}, u32[]{:S(2)}) copy-start(bf16[384,128,32]{1,2,0:T(8,128)(2,1)} %fusion.10) | copy-start | bytes 9437188
  168.5 78.7 %copy-start.9 = (f32[1,4096]{1,0:T(1,128)S(1)}, f32[1,4096]{1,0:T(1,128)}, u32[]{:S(2)}) copy-start(f32[1,4096]{1,0:T(1,128)} %param.18) | copy-start | bytes 49156
  168.5 78.7 %copy-start.10 = (f32[1,512]{1,0:T(1,128)S(1)}, f32[1,512]{1,0:T(1,128)}, u32[]{:S(2)}) copy-start(f32[1,512]{1,0:T(1,128)} %param.20) | copy-start | bytes 6148
  247.2 10.6 %copy-start.4 = (bf16[62,1024]{1,0:T(8,128)(2,1)S(1)}, bf16[62,1024]{1,0:T(8,128)(2,1)}, u32[]{:S(2)}) copy-start(bf16[62,1024]{1,0:T(8,128)(2,1)} %param.22) | copy-start | bytes 380932
  247.2 21.8 %copy-start.8 = (s32[120]{0:T(128)S(1)}, s32[120]{0:T(128)}, u32[]{:S(2)}) copy-start(s32[120]{0:T(128)} %constant.23) | copy-start | bytes 1444
  254.2 16.8 %copy-start.5 = (bf16[96,128]{1,0:T(8,128)(2,1)S(1)}, bf16[96,128]{1,0:T(8,128)(2,1)}, u32[]{:S(2)}) copy-start(bf16[96,128]{1,0:T(8,128)(2,1)} %param.21) | copy-start | bytes 73732
  254.2 16.8 %copy-start.6 = (f32[1024]{0:T(1024)S(1)}, f32[1024]{0:T(1024)}, u32[]{:S(2)}) copy-start(f32[1024]{0:T(1024)} %param.23) | copy-start | bytes 12292
  254.2 14.8 %all-to-all-start.2 = ((bf16[4,96,512]{2,1,0:T(8,128)(2,1)}), bf16[4,96,512]{2,1,0:T(8,128)(2,1)S(1)}, u32[]{:S(2)}, u32[]{:S(2)}) async-start(bf16[4,96,512]{2,1,0:T(8,128)(2,1)} %bitcast.14), calls=%async_computation.2 | async-start | bytes 786432 | tf_op jit(solution)/shard_map/all_to_all | solution.py:55
Sparse Core Ops, SparseCore 0:
  8.9 80.3 all-gather.7
  90.9 74.7 all-gather.9
  167.3 79.9 all-gather.11
where the time goes:
time: 279 us
  waiting for transfers between devices  205 us (73%)
  local copies, waits for them, and re-layouts  20.4 us (7%)
  matrix products  14.6 us (5%)
  starting transfers between devices  13.7 us (5%)
  between operations  13.3 us (5%)
  blocking collectives  11.1 us (4%)
    all_gather x1, waiting for transfers between devices, on_device(): lax.all_gather(compress_weight[0], 'feat', axis=0, tiled=True)  74.9 us
    all_to_all x1, waiting for transfers between devices, on_device(): lax.all_to_all(pooled_second, 'feat', split_axis=2, concat_axis=1, tiled=...  69.1 us
    all_to_all x1, waiting for transfers between devices, on_device(): lax.all_to_all(pooled_first, 'feat', split_axis=2, concat_axis=1, tiled=T...  59.2 us
    unnamed x25, local copies, waits for them, and re-layouts  16.6 us
    all_gather x1, blocking collectives, on_device(): weight_piece = lax.all_gather(mlp_weight, 'tower', axis=0, tiled=True)  11.1 us
    dot_general x1, matrix products, on_device(): jnp.dot(crossed, squeeze_piece, preferred_element_type=jnp.float32)  6.96 us
    all_to_all x1, starting transfers between devices, on_device(): lax.all_to_all(pooled_first, 'feat', split_axis=2, concat_axis=1, tiled=T...  6.32 us
  transfers between devices with their start and end apart: 6, of which 3 were waited for; matrix products, arithmetic and copies ran while one was open for 9% of the time, Pallas kernels for 0%

commit v1 on v0

--- a/solution.py
+++ b/solution.py
@@ -4,6 +4,18 @@
 import numpy as np
 from jax import lax
 from jax.sharding import PartitionSpec as P
+
+
+def rotated_exchange(x, axis, split, join):
+    ways, here = (lax.axis_size(axis), lax.axis_index(axis))
+    width = x.shape[split] // ways
+    turned = jnp.roll(x, -here * width, axis=split)
+    got = [lax.slice_in_dim(turned, 0, width, axis=split)]
+    for far in range(1, ways):
+        sent = lax.slice_in_dim(turned, far * width, (far + 1) * width, axis=split)
+        got.append(lax.ppermute(sent, axis, [(d, (d + far) % ways) for d in range(ways)]))
+    line = jnp.concatenate(got[::-1], axis=join)
+    return jnp.roll(line, (here + 1) * got[0].shape[join], axis=join)
 
 
 def pair_positions(vector_count):
@@ -25,7 +37,7 @@
     mlp_bias,
 ):
     group_one, group_two = (
-        lax.all_to_all(pooled_first, "feat", split_axis=2, concat_axis=1, tiled=True),
+        rotated_exchange(pooled_first, "feat", 2, 1),
         lax.all_to_all(pooled_second, "feat", split_axis=2, concat_axis=1, tiled=True),
     )
     slot_data = jnp.concatenate([group_one[0], group_two[0]], 0)

time: 279 us -> 271 us (0.971)
  waiting for transfers between devices: 205 us -> 197 us
  local copies, waits for them, and re-layouts: 20.4 us -> 17.2 us
    ppermute x0 -> x3, waiting for transfers between devices: none -> 110 us  [rotated_exchange(): lax.ppermute(sent, axis, [(d, (d + far) % ways) for d in range(ways)])]
    all_to_all x1, waiting for transfers between devices: 69.1 us -> 0.01 us  [on_device(): lax.all_to_all(pooled_second, 'feat', split_axis=2, concat_axis=1, tiled=...]
    all_to_all x1 -> x0, waiting for transfers between devices: 59.2 us -> none  [on_device(): lax.all_to_all(pooled_first, 'feat', split_axis=2, concat_axis=1, tiled=T...]
    all_to_all x1 -> x0, starting transfers between devices: 6.32 us -> none  [on_device(): lax.all_to_all(pooled_first, 'feat', split_axis=2, concat_axis=1, tiled=T...]
    all_gather x1, waiting for transfers between devices: 74.9 us -> 80.8 us  [on_device(): lax.all_gather(compress_weight[0], 'feat', axis=0, tiled=True)]
    ppermute x0 -> x3, starting transfers between devices: none -> 4.91 us  [rotated_exchange(): lax.ppermute(sent, axis, [(d, (d + far) % ways) for d in range(ways)])]
    all_gather x1, waiting for transfers between devices: 0.02 us -> 3.94 us  [on_device(): up_piece = lax.all_gather(cross_up[0], 'feat', axis=0, tiled=True)]
    unnamed x25 -> x27, local copies, waits for them, and re-layouts: 16.6 us -> 12.7 us
  transfers between devices with their start and end apart: 6 -> 8, of which waited for: 3 -> 4; matrix products, arithmetic and copies ran while one was open for 9% -> 9% of each run, Pallas kernels for 0% -> 0%
where the time goes in v1:
time: 271 us
  waiting for transfers between devices  197 us (73%)
  local copies, waits for them, and re-layouts  17.2 us (6%)
  starting transfers between devices  14.9 us (5%)
  matrix products  14.6 us (5%)
  between operations  13.3 us (5%)
  blocking collectives  11.1 us (4%)
    ppermute x3, waiting for transfers between devices, rotated_exchange(): lax.ppermute(sent, axis, [(d, (d + far) % ways) for d in range(ways)])  110 us
    all_gather x1, waiting for transfers between devices, on_device(): lax.all_gather(compress_weight[0], 'feat', axis=0, tiled=True)  80.8 us
    unnamed x27, local copies, waits for them, and re-layouts  12.7 us
    all_gather x1, blocking collectives, on_device(): weight_piece = lax.all_gather(mlp_weight, 'tower', axis=0, tiled=True)  11.1 us
    dot_general x1, matrix products, on_device(): jnp.dot(crossed, squeeze_piece, preferred_element_type=jnp.float32)  6.96 us
    all_to_all x1, starting transfers between devices, on_device(): lax.all_to_all(pooled_second, 'feat', split_axis=2, concat_axis=1, tiled=...  6.32 us
  transfers between devices with their start and end apart: 8, of which 4 were waited for; matrix products, arithmetic and copies ran while one was open for 9% of the time, Pallas kernels for 0%

profile of v1, /device:TPU:0, one launch (start us, length us, event | category | flops | bytes accessed | tf_op | source)
XLA Modules:
  0.0 270.9 jit_solution(6861667365991207996)
XLA Ops:
  6.5 0.7 all-gather.8.cloned.1.call-update
  7.3 0.7 all-gather.10.cloned.1.call-update
  8.8 8.2 %copy.25 = bf16[1,4,1536,128]{3,1,0,2:T(4,128)(2,1)} copy(bf16[1,4,1536,128]{3,2,1,0:T(8,128)(2,1)S(1)} %copy-done.1) | data formatting | bytes 3145728 | tf_op args[1]
  17.0 6.3 %all-to-all-start = ((bf16[1,4,1536,128]{3,1,0,2:T(4,128)(2,1)}), bf16[1,4,1536,128]{3,1,0,2:T(4,128)(2,1)S(1)}, u32[]{:S(2)}, u32[]{:S(2)}) async-start(bf16[1,4,1536,128]{3,1,0,2:T(4,128)(2,1)} %copy.25), calls=%async_computation | async-start | bytes 3145728 | tf_op jit(solution)/shard_map/all_to_all | solution.py:41
  23.3 2.5 fusion.15
  25.8 1.1 fusion.39
  26.9 3.8 %collective-permute-start = (bf16[1,4,384,128]{3,2,1,0:T(8,128)(2,1)}, bf16[1,4,384,128]{3,2,1,0:T(8,128)(2,1)S(1)}, u32[]{:S(2)}, u32[]{:S(2)}) collective-permute-start(bf16[1,4,384,128]{3,2,1,0:T(8,128)(2,1)} %get-tuple-element.7), channel_id=1, source_target_pairs={{0,12},{4,0},{8,4},{12,8},{1,13},{5,1},{9,5},{13,9},{2,14},{6,2},{... | collective-permute-start | bytes 1179656 | tf_op jit(solution)/shard_map/ppermute | solution.py:16
  30.8 1.1 collective-permute-start.2
  31.9 55.9 %collective-permute-done = bf16[1,4,384,128]{3,2,1,0:T(8,128)(2,1)S(1)} collective-permute-done((bf16[1,4,384,128]{3,2,1,0:T(8,128)(2,1)}, bf16[1,4,384,128]{3,2,1,0:T(8,128)(2,1)S(1)}, u32[]{:S(2)}, u32[]{:S(2)}) %collective-permute-start) | collective-permute-done | bytes 393248 | tf_op jit(solution)/shard_map/ppermute | solution.py:16
  87.8 54.4 %collective-permute-done.1 = bf16[1,4,384,128]{3,2,1,0:T(8,128)(2,1)} collective-permute-done((bf16[1,4,384,128]{3,2,1,0:T(8,128)(2,1)}, bf16[1,4,384,128]{3,2,1,0:T(8,128)(2,1)}, u32[]{:S(2)}, u32[]{:S(2)}) %collective-permute-start.1) | collective-permute-done | bytes 393248 | tf_op jit(solution)/shard_map/ppermute | solution.py:16
  142.2 1.0 constant_dynamic-update-slice_fusion.4
  143.3 1.0 constant_dynamic-update-slice_fusion.3
  144.5 1.0 constant_dynamic-update-slice_fusion.1
  145.5 1.0 constant_dynamic-update-slice_fusion
  146.8 1.0 copy.41
  148.4 2.6 fusion.10
  151.1 3.8 %fusion.24 = bf16[384,256]{1,0:T(8,128)(2,1)S(1)} fusion(bf16[1,4096,256]{2,1,0:T(8,128)(2,1)} %all-gather.8.cloned.1.call-done, bf16[48,8,32,128]{3,2,1,0:T(8,128)(2,1)} %bitcast.54), kind=kOutput, calls=%fused_computation.25 | convolution fusion | flops 805404672 | bytes 5439488 | tf_op jit(solution)/shard_map/dot_general | solution.py:55
  154.9 3.9 %all-gather.10.cloned.1.call-done = bf16[1,4096,256]{2,1,0:T(8,128)(2,1)} async-done(((bf16[1,1024,256]{2,1,0:T(8,128)(2,1)}), bf16[1,4096,256]{2,1,0:T(8,128)(2,1)}) %all-gather.10.cloned.1.call-update) | async-done | bytes 2097168 | tf_op jit(solution)/shard_map/all_gather | solution.py:58
  158.8 80.8 %all-gather.12.cloned.1.call-done = bf16[1,4096,512]{2,1,0:T(8,128)(2,1)} async-done(((bf16[1,1024,512]{2,1,0:T(8,128)(2,1)}), bf16[1,4096,512]{2,1,0:T(8,128)(2,1)}) %all-gather.12.cloned.1.call-update) | async-done | bytes 4194320 | tf_op jit(solution)/shard_map/all_gather | solution.py:59
  239.6 7.0 %fusion.19 = bf16[384,512]{1,0:T(8,128)(2,1)} fusion(bf16[1,4096,512]{2,1,0:T(8,128)(2,1)} %all-gather.12.cloned.1.call-done, bf16[384,256]{1,0:T(8,128)(2,1)S(1)} %fusion.24, f32[4096]{0:T(1024)S(1)} %bitcast.61, bf16[48,8,32,128]{3,2,1,0:T(8,128)(2,1)S(1)} %bitcast.55, bf16[1,4096,256]{2,1,0:T(8,128)(2,1)} %all-gather.10.cloned.1.call-done, ...), kind=kOutput, calls=%fused_computation.21 | convolution fusion | flops 2424176640 | bytes 10045440 | tf_op jit(solution)/shard_map/dot_general | solution.py:65
  246.6 3.6 %all-to-all-start.1 = ((bf16[4,96,512]{2,1,0:T(8,128)(2,1)}), bf16[4,96,512]{2,1,0:T(8,128)(2,1)S(1)}, u32[]{:S(2)}, u32[]{:S(2)}) async-start(bf16[4,96,512]{2,1,0:T(8,128)(2,1)} %bitcast.12), calls=%async_computation.1 | async-start | bytes 786432 | tf_op jit(solution)/shard_map/all_to_all | solution.py:67
  250.2 11.1 %all-gather.3 = bf16[4,62,1024]{2,1,0:T(8,128)(2,1)S(1)} all-gather(bf16[1,62,1024]{2,1,0:T(8,128)(2,1)S(1)} %bitcast.58), channel_id=1, replica_groups=mesh['groups'=2,'feat'=4,'tower'=4] {'tower'}, dimensions={0}, use_global_device_ids=true | all-gather | bytes 634880 | tf_op jit(solution)/shard_map/all_gather | solution.py:79
  262.6 0.7 gather_fusion
  263.4 0.9 fusion.23
  (40 shorter events, 3.1 us)
Async XLA Ops:
  6.5 2.2 copy-start.1
  6.5 144.5 %all-gather.8.cloned.1.call-start = ((), (), s32[]{:S(2)}) async-start(), calls=%async_computation.2 | async-start | bytes 2621440 | tf_op jit(solution)/shard_map/all_gather | solution.py:53
  7.3 151.5 %all-gather.10.cloned.1.call-start = ((), (), s32[]{:S(2)}) async-start(), calls=%async_computation.3 | async-start | bytes 2621440 | tf_op jit(solution)/shard_map/all_gather | solution.py:58
  8.0 231.6 %all-gather.12.cloned.1.call-start = ((), (), s32[]{:S(2)}) async-start(), calls=%async_computation.4 | async-start | bytes 5242880 | tf_op jit(solution)/shard_map/all_gather | solution.py:59
  17.0 130.9 %all-to-all-start = ((bf16[1,4,1536,128]{3,1,0,2:T(4,128)(2,1)}), bf16[1,4,1536,128]{3,1,0,2:T(4,128)(2,1)S(1)}, u32[]{:S(2)}, u32[]{:S(2)}) async-start(bf16[1,4,1536,128]{3,1,0,2:T(4,128)(2,1)} %copy.25), calls=%async_computation | async-start | bytes 3145728 | tf_op jit(solution)/shard_map/all_to_all | solution.py:41
  26.9 60.8 %collective-permute-start = (bf16[1,4,384,128]{3,2,1,0:T(8,128)(2,1)}, bf16[1,4,384,128]{3,2,1,0:T(8,128)(2,1)S(1)}, u32[]{:S(2)}, u32[]{:S(2)}) collective-permute-start(bf16[1,4,384,128]{3,2,1,0:T(8,128)(2,1)} %get-tuple-element.7), channel_id=1, source_target_pairs={{0,12},{4,0},{8,4},{12,8},{1,13},{5,1},{9,5},{13,9},{2,14},{6,2},{... | collective-permute-start | bytes 1179656 | tf_op jit(solution)/shard_map/ppermute | solution.py:16
  30.8 111.5 %collective-permute-start.1 = (bf16[1,4,384,128]{3,2,1,0:T(8,128)(2,1)}, bf16[1,4,384,128]{3,2,1,0:T(8,128)(2,1)}, u32[]{:S(2)}, u32[]{:S(2)}) collective-permute-start(bf16[1,4,384,128]{3,2,1,0:T(8,128)(2,1)} %get-tuple-element.6), channel_id=1, source_target_pairs={{0,8},{4,12},{8,0},{12,4},{1,9},{5,13},{9,1},{13,5},{2,10},{6,14},... | collective-permute-start | bytes 1179656 | tf_op jit(solution)/shard_map/ppermute | solution.py:16
  30.8 112.5 %collective-permute-start.2 = (bf16[1,4,384,128]{3,2,1,0:T(8,128)(2,1)}, bf16[1,4,384,128]{3,2,1,0:T(8,128)(2,1)}, u32[]{:S(2)}, u32[]{:S(2)}) collective-permute-start(bf16[1,4,384,128]{3,2,1,0:T(8,128)(2,1)} %get-tuple-element.5), channel_id=1, source_target_pairs={{0,4},{4,8},{8,12},{12,0},{1,5},{5,9},{9,13},{13,1},{2,6},{6,10},{... | collective-permute-start | bytes 1179656 | tf_op jit(solution)/shard_map/ppermute | solution.py:16
  146.8 1.6 copy-start.5
  151.1 88.5 %copy-start = (bf16[384,128,32]{1,2,0:T(8,128)(2,1)S(1)}, bf16[384,128,32]{1,2,0:T(8,128)(2,1)}, u32[]{:S(2)}) copy-start(bf16[384,128,32]{1,2,0:T(8,128)(2,1)} %fusion.10) | copy-start | bytes 9437188
  151.1 88.5 %copy-start.7 = (f32[1,4096]{1,0:T(1,128)S(1)}, f32[1,4096]{1,0:T(1,128)}, u32[]{:S(2)}) copy-start(f32[1,4096]{1,0:T(1,128)} %param.18) | copy-start | bytes 49156
  151.1 88.5 %copy-start.8 = (f32[1,512]{1,0:T(1,128)S(1)}, f32[1,512]{1,0:T(1,128)}, u32[]{:S(2)}) copy-start(f32[1,512]{1,0:T(1,128)} %param.20) | copy-start | bytes 6148
  239.6 10.6 %copy-start.2 = (bf16[62,1024]{1,0:T(8,128)(2,1)S(1)}, bf16[62,1024]{1,0:T(8,128)(2,1)}, u32[]{:S(2)}) copy-start(bf16[62,1024]{1,0:T(8,128)(2,1)} %param.22) | copy-start | bytes 380932
  239.6 21.8 %copy-start.6 = (s32[120]{0:T(128)S(1)}, s32[120]{0:T(128)}, u32[]{:S(2)}) copy-start(s32[120]{0:T(128)} %constant.72) | copy-start | bytes 1444
  246.6 16.8 %copy-start.3 = (bf16[96,128]{1,0:T(8,128)(2,1)S(1)}, bf16[96,128]{1,0:T(8,128)(2,1)}, u32[]{:S(2)}) copy-start(bf16[96,128]{1,0:T(8,128)(2,1)} %param.21) | copy-start | bytes 73732
  246.6 16.8 %copy-start.4 = (f32[1024]{0:T(1024)S(1)}, f32[1024]{0:T(1024)}, u32[]{:S(2)}) copy-start(f32[1024]{0:T(1024)} %param.23) | copy-start | bytes 12292
  246.6 14.8 %all-to-all-start.1 = ((bf16[4,96,512]{2,1,0:T(8,128)(2,1)}), bf16[4,96,512]{2,1,0:T(8,128)(2,1)S(1)}, u32[]{:S(2)}, u32[]{:S(2)}) async-start(bf16[4,96,512]{2,1,0:T(8,128)(2,1)} %bitcast.12), calls=%async_computation.1 | async-start | bytes 786432 | tf_op jit(solution)/shard_map/all_to_all | solution.py:67
Sparse Core Ops, SparseCore 0:
  8.9 80.4 all-gather.7
  91.0 67.8 all-gather.9
  160.4 79.1 all-gather.11
